TPU v7x, 256 devices: a whole 4x4x8 slice. The times are simulated.
256 devices in a mesh: col: 32 (over z, x), row: 8 (over y, core).
Axes of the slice: x: 4, y: 4, z: 8, core: 2. Of those that a mesh axis runs over, the one named last changes fastest.
Arguments:
- right_side: float32 [6, 64, 64, 128], P(None, 'row'), may hold values from -6 to 6
- lower_blocks: bfloat16 [15, 64, 64, 128, 128], P(None, 'row', 'col'), may hold values from -0.078125 to 0.078125
- pattern: int32 [15, 64, 64], P(None, 'row', 'col'), may hold values 0 or 1
- diag_inverse: bfloat16 [6, 64, 128, 128], P(None, 'row'), may hold values from -2 to 2
Outputs:
- solution: float32 [6, 64, 64, 128], P(None, 'col')
All inputs are finite; a program needn't handle non-finite values. No bound on the sum of `pattern` on one device may be relied on, other than what follows from the above.
Results may differ from a plain program's by a relative error of at most 0.0029.
Values sent between devices are 32-bit elements; how exact they have to be, the bound alone decides.
No kernel may reach another device: no remote copies, remote signals or barrier semaphores. Data moves between devices by JAX's collectives and lax.ppermute only.
A program may use at most 64 MiB of HBM per device.

v0:
```python
import jax
import jax.numpy as jnp
from jax import lax
from jax.sharding import PartitionSpec as P


def broadcast(shard, axis, root):
    mine = lax.axis_index(axis) == root
    return lax.psum(jnp.where(mine, shard, jnp.zeros_like(shard)), axis)


def solve_rows(residual, inverse):
    return jnp.einsum(
        "pnb,pbd->pnd", residual, inverse.astype(jnp.float32), precision=lax.Precision.HIGHEST
    )


def body(right_side, lower_blocks, pattern, diag_inverse):
    row_count = right_side.shape[1]
    col_count = pattern.shape[2]
    col_id = lax.axis_index("col")
    source = col_id * col_count // row_count
    first_row = col_id * col_count - source * row_count
    solved = []
    outputs = []
    for section in range(right_side.shape[0]):
        rhs_section = right_side[section]
        inv_section = diag_inverse[section]
        if section > 0:
            offset = section * (section - 1) // 2
            blocks = lower_blocks[offset : offset + section]
            weights = pattern[offset : offset + section].astype(jnp.float32)
            earlier = jnp.stack(solved)
            products = jnp.einsum(
                "lcnb,lrcbd->lrcnd", earlier, blocks, preferred_element_type=jnp.float32
            )
            partial_value = jnp.sum(weights[:, :, :, None, None] * products, axis=(0, 2))
            totals = lax.psum(partial_value, "col")
            row_solved = solve_rows(rhs_section - totals, inv_section)
            owned = lax.dynamic_slice_in_dim(row_solved, first_row, col_count, 0)
        else:
            owned_rhs = lax.dynamic_slice_in_dim(rhs_section, first_row, col_count, 0)
            owned_inv = lax.dynamic_slice_in_dim(inv_section, first_row, col_count, 0)
            owned = solve_rows(owned_rhs, owned_inv)
        segment = broadcast(owned, "row", source)
        outputs.append(segment)
        solved.append(segment.astype(jnp.bfloat16))
    return jnp.stack(outputs)


def solution(mesh):
    placed = (
        P(None, "row", None, None),
        P(None, "row", "col", None, None),
        P(None, "row", "col"),
        P(None, "row", None, None),
    )
    return jax.shard_map(
        body, mesh=mesh, in_specs=placed, out_specs=P(None, "col", None, None), check_vma=False
    )
```

profile of v0, /device:TPU:2, one launch (start us, length us, event | category | flops | bytes accessed | tf_op | source)
XLA Modules:
  0.0 1147.2 jit_solution(12751743245303424274)
XLA Ops:
  6.5 1.1 slice.66
  7.6 1.0 slice.67
  8.6 0.8 convolution_select_fusion
  9.4 0.0 all-reduce.12.cloned.1.call-update
  9.5 0.0 all-reduce.14.cloned.1.call-start
  9.5 0.8 copy.32
  10.3 67.2 %all-reduce.12.cloned.1.call-done = f32[2,64,128]{2,1,0:T(8,128)} async-done(((f32[2,64,128]{2,1,0:T(8,128)}), f32[2,64,128]{2,1,0:T(8,128)}) %all-reduce.12.cloned.1.call-update) | async-done | bytes 65552 | tf_op jit(solution)/shard_map/psum | solution.py:9
  77.6 2.1 fusion.12
  79.6 0.0 all-reduce.14.cloned.1.call-update
  79.6 0.0 all-reduce.16.cloned.1.call-start
  79.7 0.1 slice.73
  79.8 0.1 copy.34
  79.9 0.1 copy.20
  80.0 144.3 %all-reduce.14.cloned.1.call-done = f32[8,64,128]{2,1,0:T(8,128)} async-done(((f32[8,64,128]{2,1,0:T(8,128)}), f32[8,64,128]{2,1,0:T(8,128)}) %all-reduce.14.cloned.1.call-update) | async-done | bytes 262160 | tf_op jit(solution)/shard_map/psum | solution.py:38
  224.3 1.4 fusion.28
  225.6 0.6 dynamic-slice_select_fusion.3
  226.3 0.0 all-reduce.18.cloned.1.call-start
  226.4 63.3 %all-reduce.16.cloned.1.call-done = f32[2,64,128]{2,1,0:T(8,128)} async-done(((f32[2,64,128]{2,1,0:T(8,128)}), f32[2,64,128]{2,1,0:T(8,128)}) %all-reduce.16.cloned.1.call-update) | async-done | bytes 65552 | tf_op jit(solution)/shard_map/psum | solution.py:9
  289.7 0.9 constant_dynamic-update-slice_fusion.2
  290.6 2.2 fusion.10
  292.9 0.0 all-reduce.20.cloned.1.call-start
  292.9 143.4 %all-reduce.18.cloned.1.call-done = f32[8,64,128]{2,1,0:T(8,128)} async-done(((f32[8,64,128]{2,1,0:T(8,128)}), f32[8,64,128]{2,1,0:T(8,128)}) %all-reduce.18.cloned.1.call-update) | async-done | bytes 262160 | tf_op jit(solution)/shard_map/psum | solution.py:38
  436.3 1.3 fusion.26
  437.6 0.6 dynamic-slice_select_fusion.2
  438.3 0.0 all-reduce.22.cloned.1.call-start
  438.3 0.1 slice.77
  438.4 0.1 copy.35
  438.5 0.1 copy.22
  438.6 63.0 %all-reduce.20.cloned.1.call-done = f32[2,64,128]{2,1,0:T(8,128)} async-done(((f32[2,64,128]{2,1,0:T(8,128)}), f32[2,64,128]{2,1,0:T(8,128)}) %all-reduce.20.cloned.1.call-update) | async-done | bytes 65552 | tf_op jit(solution)/shard_map/psum | solution.py:9
  501.6 0.9 constant_dynamic-update-slice_fusion.1
  502.5 2.5 fusion.6
  505.0 0.0 all-reduce.24.cloned.1.call-start
  505.1 143.3 %all-reduce.22.cloned.1.call-done = f32[8,64,128]{2,1,0:T(8,128)} async-done(((f32[8,64,128]{2,1,0:T(8,128)}), f32[8,64,128]{2,1,0:T(8,128)}) %all-reduce.22.cloned.1.call-update) | async-done | bytes 262160 | tf_op jit(solution)/shard_map/psum | solution.py:38
  648.4 1.3 fusion.24
  649.7 0.6 dynamic-slice_select_fusion.1
  650.4 0.0 all-reduce.26.cloned.1.call-start
  650.4 0.1 slice.81
  650.5 0.1 copy.36
  650.6 0.1 copy.24
  650.7 63.2 %all-reduce.24.cloned.1.call-done = f32[2,64,128]{2,1,0:T(8,128)} async-done(((f32[2,64,128]{2,1,0:T(8,128)}), f32[2,64,128]{2,1,0:T(8,128)}) %all-reduce.24.cloned.1.call-update) | async-done | bytes 65552 | tf_op jit(solution)/shard_map/psum | solution.py:9
  713.9 0.9 constant_dynamic-update-slice_fusion
  714.7 2.8 fusion.3
  717.5 0.0 all-reduce.28.cloned.1.call-start
  717.6 0.1 slice.85
  717.6 0.1 copy.37
  717.7 0.1 copy.26
  717.8 0.6 bitcast_dynamic-update-slice_fusion.4
  718.5 142.5 %all-reduce.26.cloned.1.call-done = f32[8,64,128]{2,1,0:T(8,128)} async-done(((f32[8,64,128]{2,1,0:T(8,128)}), f32[8,64,128]{2,1,0:T(8,128)}) %all-reduce.26.cloned.1.call-update) | async-done | bytes 262160 | tf_op jit(solution)/shard_map/psum | solution.py:38
  860.9 1.3 fusion.22
  862.2 0.6 dynamic-slice_select_fusion
  862.9 0.0 all-reduce.30.cloned.1.call-start
  862.9 0.6 bitcast_dynamic-update-slice_fusion.3
  863.6 62.8 %all-reduce.28.cloned.1.call-done = f32[2,64,128]{2,1,0:T(8,128)} async-done(((f32[2,64,128]{2,1,0:T(8,128)}), f32[2,64,128]{2,1,0:T(8,128)}) %all-reduce.28.cloned.1.call-update) | async-done | bytes 65552 | tf_op jit(solution)/shard_map/psum | solution.py:9
  926.4 0.9 bitcast_dynamic-update-slice_fusion.5
  927.3 3.0 fusion
  930.3 0.0 all-reduce.32.cloned.1.call-start
  930.4 0.6 bitcast_dynamic-update-slice_fusion.2
  931.0 0.6 bitcast_dynamic-update-slice_fusion.1
  931.6 142.1 %all-reduce.30.cloned.1.call-done = f32[8,64,128]{2,1,0:T(8,128)} async-done(((f32[8,64,128]{2,1,0:T(8,128)}), f32[8,64,128]{2,1,0:T(8,128)}) %all-reduce.30.cloned.1.call-update) | async-done | bytes 262160 | tf_op jit(solution)/shard_map/psum | solution.py:38
  1073.7 1.3 fusion.20
  1075.0 0.6 select_bitcast_fusion
  1075.7 0.6 bitcast_dynamic-update-slice_fusion
  1076.3 62.9 %all-reduce.32.cloned.1.call-done = f32[1,2,64,128]{3,2,1,0:T(8,128)} async-done(((f32[1,2,64,128]{3,2,1,0:T(8,128)}), f32[1,2,64,128]{3,2,1,0:T(8,128)}) %all-reduce.32.cloned.1.call-update) | async-done | bytes 65552 | tf_op jit(solution)/shard_map/psum | solution.py:9
  1139.2 1.5 constant_dynamic-update-slice_fusion.4
  (32 shorter events, 0.2 us)
Async XLA Ops:
  6.5 217.7 %copy-start = (bf16[6,8,128,128]{3,2,1,0:T(8,128)(2,1)S(1)}, bf16[6,8,128,128]{3,2,1,0:T(8,128)(2,1)}, u32[]{:S(2)}) copy-start(bf16[6,8,128,128]{3,2,1,0:T(8,128)(2,1)} %param.7) | copy-start | bytes 4718596
  6.5 73.1 %copy-start.7 = (s32[15,8,2]{0,2,1:T(2,128)S(1)}, s32[15,8,2]{0,2,1:T(2,128)}, u32[]{:S(2)}) copy-start(s32[15,8,2]{0,2,1:T(2,128)} %param.6) | copy-start | bytes 2884
  6.5 71.0 %all-reduce.12.cloned.1.call-start = ((), (), s32[]{:S(2)}) async-start(), calls=%async_computation | async-start | bytes 131072 | tf_op jit(solution)/shard_map/psum | solution.py:9
  9.5 214.8 %all-reduce.14.cloned.1.call-start = ((), (), s32[]{:S(2)}) async-start(), calls=%async_computation.1 | async-start | bytes 524288 | tf_op jit(solution)/shard_map/psum | solution.py:38
  77.6 148.8 %copy-start.2 = (f32[2,64,128]{2,1,0:T(8,128)S(1)}, f32[2,64,128]{2,1,0:T(8,128)}, u32[]{:S(2)}) copy-start(f32[2,64,128]{2,1,0:T(8,128)} %all-reduce.12.cloned.1.call-done) | copy-start | bytes 196612
  79.6 210.1 %all-reduce.16.cloned.1.call-start = ((), (), s32[]{:S(2)}) async-start(), calls=%async_computation.2 | async-start | bytes 131072 | tf_op jit(solution)/shard_map/psum | solution.py:9
  80.0 356.4 %copy-start.1 = (f32[6,8,64,128]{3,2,1,0:T(8,128)S(1)}, f32[6,8,64,128]{3,2,1,0:T(8,128)}, u32[]{:S(2)}) copy-start(f32[6,8,64,128]{3,2,1,0:T(8,128)} %param.4) | copy-start | bytes 4718596
  226.3 210.0 %all-reduce.18.cloned.1.call-start = ((), (), s32[]{:S(2)}) async-start(), calls=%async_computation.3 | async-start | bytes 524288 | tf_op jit(solution)/shard_map/psum | solution.py:38
  292.9 208.8 %all-reduce.20.cloned.1.call-start = ((), (), s32[]{:S(2)}) async-start(), calls=%async_computation.4 | async-start | bytes 131072 | tf_op jit(solution)/shard_map/psum | solution.py:9
  438.3 210.1 %all-reduce.22.cloned.1.call-start = ((), (), s32[]{:S(2)}) async-start(), calls=%async_computation.5 | async-start | bytes 524288 | tf_op jit(solution)/shard_map/psum | solution.py:38
  505.0 208.8 %all-reduce.24.cloned.1.call-start = ((), (), s32[]{:S(2)}) async-start(), calls=%async_computation.6 | async-start | bytes 131072 | tf_op jit(solution)/shard_map/psum | solution.py:9
  650.4 210.6 %all-reduce.26.cloned.1.call-start = ((), (), s32[]{:S(2)}) async-start(), calls=%async_computation.7 | async-start | bytes 524288 | tf_op jit(solution)/shard_map/psum | solution.py:38
  717.5 145.5 %copy-start.3 = (f32[2,64,128]{2,1,0:T(8,128)S(1)}, f32[2,64,128]{2,1,0:T(8,128)}, u32[]{:S(2)}) copy-start(f32[2,64,128]{2,1,0:T(8,128)} %all-reduce.16.cloned.1.call-done) | copy-start | bytes 196612
  717.5 208.9 %all-reduce.28.cloned.1.call-start = ((), (), s32[]{:S(2)}) async-start(), calls=%async_computation.8 | async-start | bytes 131072 | tf_op jit(solution)/shard_map/psum | solution.py:9
  862.9 210.8 %all-reduce.30.cloned.1.call-start = ((), (), s32[]{:S(2)}) async-start(), calls=%async_computation.9 | async-start | bytes 524288 | tf_op jit(solution)/shard_map/psum | solution.py:38
  927.3 3.1 copy-start.4
  927.3 3.8 copy-start.5
  930.3 145.4 %copy-start.6 = (f32[2,64,128]{2,1,0:T(8,128)S(1)}, f32[2,64,128]{2,1,0:T(8,128)}, u32[]{:S(2)}) copy-start(f32[2,64,128]{2,1,0:T(8,128)} %all-reduce.28.cloned.1.call-done) | copy-start | bytes 196612
  930.3 208.9 %all-reduce.32.cloned.1.call-start = ((), (), s32[]{:S(2)}) async-start(), calls=%async_computation.10 | async-start | bytes 131072 | tf_op jit(solution)/shard_map/psum | solution.py:9
Sparse Core Ops, SparseCore 0:
  9.6 67.8 all-reduce.11
  81.0 143.2 all-reduce.13
  226.6 63.0 all-reduce.15
  293.0 143.2 all-reduce.17
  438.5 63.0 all-reduce.19
  505.1 143.2 all-reduce.21
  650.7 63.0 all-reduce.23
  717.6 143.2 all-reduce.25
  863.3 63.0 all-reduce.27
  930.4 143.2 all-reduce.29
  1076.0 63.0 all-reduce.31
where the time goes:
time: 1150 us
  waiting for transfers between devices  1100 us (96%)
  matrix products  19.9 us (2%)
  between operations  13.4 us (1%)
    psum x5, waiting for transfers between devices, body(): totals = lax.psum(partial_value, 'col')  716 us
    psum x6, waiting for transfers between devices, broadcast(): return lax.psum(jnp.where(mine, shard, jnp.zeros_like(shard)), axis)  382 us
  transfers between devices with their start and end apart: 11, of which 11 were waited for; matrix products, arithmetic and copies ran while one was open for 0% of the time, Pallas kernels for 0%

commit v1 on v0

--- a/solution.py
+++ b/solution.py
@@ -4,9 +4,15 @@
 from jax.sharding import PartitionSpec as P
 
 
+def summed_here(x, mesh_axis):
+    parts = lax.all_gather(x, mesh_axis, axis=0, tiled=False)
+    summed = parts.sum(axis=0)
+    return summed
+
+
 def broadcast(shard, axis, root):
     mine = lax.axis_index(axis) == root
-    return lax.psum(jnp.where(mine, shard, jnp.zeros_like(shard)), axis)
+    return summed_here(jnp.where(mine, shard, jnp.zeros_like(shard)), axis)
 
 
 def solve_rows(residual, inverse):

time: 1150 us -> 835 us (0.73)
  waiting for transfers between devices: 1100 us -> 714 us
  blocking collectives: 0 us -> 80.9 us
    psum x6 -> x0, waiting for transfers between devices: 382 us -> none  [broadcast(): return lax.psum(jnp.where(mine, shard, jnp.zeros_like(shard)), axis)]
    all_gather x0 -> x6, blocking collectives: none -> 80.9 us  [summed_here(): parts = lax.all_gather(x, mesh_axis, axis=0, tiled=False)]
  transfers between devices with their start and end apart: 11 -> 5, of which waited for: 11 -> 5; matrix products, arithmetic and copies ran while one was open for 0% -> 0% of each run, Pallas kernels for 0% -> 0%
where the time goes in v1:
time: 835 us; the launch traced here: 832 us
  waiting for transfers between devices  714 us (86%)
  blocking collectives  80.9 us (10%)
  matrix products  19.5 us (2%)
  between operations  13.3 us (2%)
    psum x5, waiting for transfers between devices, body(): totals = lax.psum(partial_value, 'col')  714 us
    all_gather x6, blocking collectives, summed_here(): parts = lax.all_gather(x, mesh_axis, axis=0, tiled=False)  80.9 us
  transfers between devices with their start and end apart: 5, of which 5 were waited for; matrix products, arithmetic and copies ran while one was open for 0% of the time, Pallas kernels for 0%

profile of v1, /device:TPU:2, one launch (start us, length us, event | category | flops | bytes accessed | tf_op | source)
XLA Modules:
  0.0 831.8 jit_solution(8829691211701518336)
XLA Ops:
  6.5 0.0 copy-start.1
  6.5 0.0 all-reduce.6.cloned.1.call-start
  6.5 1.0 slice.66
  7.5 0.0 copy-start
  7.5 1.1 slice.67
  8.6 0.2 convolution_select_fusion
  8.8 13.6 %all-gather = f32[16,64,128]{2,1,0:T(8,128)S(1)} all-gather(f32[2,64,128]{2,1,0:T(8,128)S(1)} %convolution_select_fusion), channel_id=2, replica_groups=mesh['col'=32,'row'=8] {'row'}, dimensions={0}, use_global_device_ids=true | all-gather | bytes 589824 | tf_op jit(solution)/shard_map/all_gather | solution.py:8
  22.5 0.0 copy-done.1
  22.5 0.1 copy.38
  22.6 2.0 fusion.12
  24.6 0.0 all-reduce.6.cloned.1.call-update
  24.6 0.0 all-reduce.8.cloned.1.call-start
  24.6 0.1 slice.73
  24.7 0.1 copy.40
  24.8 0.1 copy.26
  24.9 146.4 %all-reduce.6.cloned.1.call-done = f32[8,64,128]{2,1,0:T(8,128)} async-done(((f32[8,64,128]{2,1,0:T(8,128)}), f32[8,64,128]{2,1,0:T(8,128)}) %all-reduce.6.cloned.1.call-update) | async-done | bytes 262160 | tf_op jit(solution)/shard_map/psum | solution.py:44
  171.3 0.0 copy-done
  171.3 1.4 fusion.28
  172.7 13.4 %all-gather.1 = f32[16,64,128]{2,1,0:T(8,128)S(1)} all-gather(f32[2,64,128]{2,1,0:T(8,128)S(1)} %dynamic-slice_select_fusion.4), channel_id=3, replica_groups=mesh['col'=32,'row'=8] {'row'}, dimensions={0}, use_global_device_ids=true | all-gather | bytes 589824 | tf_op jit(solution)/shard_map/all_gather | solution.py:8
  186.2 2.2 fusion.10
  188.5 0.0 all-reduce.8.cloned.1.call-update
  188.5 0.0 all-reduce.10.cloned.1.call-start
  188.5 0.1 slice.77
  188.6 0.1 copy.41
  188.7 0.1 copy.28
  188.8 141.7 %all-reduce.8.cloned.1.call-done = f32[8,64,128]{2,1,0:T(8,128)} async-done(((f32[8,64,128]{2,1,0:T(8,128)}), f32[8,64,128]{2,1,0:T(8,128)}) %all-reduce.8.cloned.1.call-update) | async-done | bytes 262160 | tf_op jit(solution)/shard_map/psum | solution.py:44
  330.5 1.4 fusion.26
  331.9 13.4 %all-gather.2 = f32[16,64,128]{2,1,0:T(8,128)S(1)} all-gather(f32[2,64,128]{2,1,0:T(8,128)S(1)} %dynamic-slice_select_fusion.3), channel_id=4, replica_groups=mesh['col'=32,'row'=8] {'row'}, dimensions={0}, use_global_device_ids=true | all-gather | bytes 589824 | tf_op jit(solution)/shard_map/all_gather | solution.py:8
  345.4 2.5 fusion.6
  347.9 0.0 all-reduce.10.cloned.1.call-update
  348.0 0.0 all-reduce.12.cloned.1.call-start
  348.0 0.1 slice.81
  348.1 0.1 slice.85
  348.2 0.1 copy.42
  348.2 0.1 copy.30
  348.4 0.1 copy.43
  348.5 0.1 copy.32
  348.6 141.5 %all-reduce.10.cloned.1.call-done = f32[8,64,128]{2,1,0:T(8,128)} async-done(((f32[8,64,128]{2,1,0:T(8,128)}), f32[8,64,128]{2,1,0:T(8,128)}) %all-reduce.10.cloned.1.call-update) | async-done | bytes 262160 | tf_op jit(solution)/shard_map/psum | solution.py:44
  490.0 1.4 fusion.24
  491.4 13.4 %all-gather.3 = f32[16,64,128]{2,1,0:T(8,128)S(1)} all-gather(f32[2,64,128]{2,1,0:T(8,128)S(1)} %dynamic-slice_select_fusion.2), channel_id=5, replica_groups=mesh['col'=32,'row'=8] {'row'}, dimensions={0}, use_global_device_ids=true | all-gather | bytes 589824 | tf_op jit(solution)/shard_map/all_gather | solution.py:8
  504.9 2.8 fusion.3
  507.7 0.0 all-reduce.12.cloned.1.call-update
  507.7 0.0 all-reduce.14.cloned.1.call-start
  507.8 142.0 %all-reduce.12.cloned.1.call-done = f32[8,64,128]{2,1,0:T(8,128)} async-done(((f32[8,64,128]{2,1,0:T(8,128)}), f32[8,64,128]{2,1,0:T(8,128)}) %all-reduce.12.cloned.1.call-update) | async-done | bytes 262160 | tf_op jit(solution)/shard_map/psum | solution.py:44
  649.8 1.4 fusion.22
  651.2 13.4 %all-gather.4 = f32[16,64,128]{2,1,0:T(8,128)S(1)} all-gather(f32[2,64,128]{2,1,0:T(8,128)S(1)} %dynamic-slice_select_fusion.1), channel_id=6, replica_groups=mesh['col'=32,'row'=8] {'row'}, dimensions={0}, use_global_device_ids=true | all-gather | bytes 589824 | tf_op jit(solution)/shard_map/all_gather | solution.py:8
  664.7 3.0 fusion
  667.7 0.0 all-reduce.14.cloned.1.call-update
  667.7 0.0 copy-start.2
  667.7 142.0 %all-reduce.14.cloned.1.call-done = f32[8,64,128]{2,1,0:T(8,128)} async-done(((f32[8,64,128]{2,1,0:T(8,128)}), f32[8,64,128]{2,1,0:T(8,128)}) %all-reduce.14.cloned.1.call-update) | async-done | bytes 262160 | tf_op jit(solution)/shard_map/psum | solution.py:44
  809.8 1.4 fusion.20
  811.2 13.4 %all-gather.5 = f32[16,64,128]{2,1,0:T(8,128)S(1)} all-gather(f32[2,64,128]{2,1,0:T(8,128)S(1)} %dynamic-slice_select_fusion), channel_id=7, replica_groups=mesh['col'=32,'row'=8] {'row'}, dimensions={0}, use_global_device_ids=true | all-gather | bytes 589824 | tf_op jit(solution)/shard_map/all_gather | solution.py:8
  824.6 0.0 copy-done.2
  824.6 0.6 bitcast_dynamic-update-slice_fusion
  (26 shorter events, 0.4 us)
Async XLA Ops:
  6.5 15.9 %copy-start.1 = (s32[15,8,2]{0,2,1:T(2,128)S(1)}, s32[15,8,2]{0,2,1:T(2,128)}, u32[]{:S(2)}) copy-start(s32[15,8,2]{0,2,1:T(2,128)} %param.6) | copy-start | bytes 2884
  6.5 164.8 %all-reduce.6.cloned.1.call-start = ((), (), s32[]{:S(2)}) async-start(), calls=%async_computation | async-start | bytes 524288 | tf_op jit(solution)/shard_map/psum | solution.py:44
  7.5 163.8 %copy-start = (bf16[6,8,128,128]{3,2,1,0:T(8,128)(2,1)S(1)}, bf16[6,8,128,128]{3,2,1,0:T(8,128)(2,1)}, u32[]{:S(2)}) copy-start(bf16[6,8,128,128]{3,2,1,0:T(8,128)(2,1)} %param.7) | copy-start | bytes 4718596
  24.6 305.9 %all-reduce.8.cloned.1.call-start = ((), (), s32[]{:S(2)}) async-start(), calls=%async_computation.1 | async-start | bytes 524288 | tf_op jit(solution)/shard_map/psum | solution.py:44
  188.5 301.5 %all-reduce.10.cloned.1.call-start = ((), (), s32[]{:S(2)}) async-start(), calls=%async_computation.2 | async-start | bytes 524288 | tf_op jit(solution)/shard_map/psum | solution.py:44
  348.0 301.8 %all-reduce.12.cloned.1.call-start = ((), (), s32[]{:S(2)}) async-start(), calls=%async_computation.3 | async-start | bytes 524288 | tf_op jit(solution)/shard_map/psum | solution.py:44
  507.7 302.1 %all-reduce.14.cloned.1.call-start = ((), (), s32[]{:S(2)}) async-start(), calls=%async_computation.4 | async-start | bytes 524288 | tf_op jit(solution)/shard_map/psum | solution.py:44
  667.7 156.9 %copy-start.2 = (f32[6,2,64,128]{3,2,1,0:T(8,128)}, f32[6,2,64,128]{3,2,1,0:T(8,128)S(1)}, u32[]{:S(2)}) copy-start(f32[6,2,64,128]{3,2,1,0:T(8,128)S(1)} %bitcast_dynamic-update-slice_fusion.1) | copy-start | bytes 1179652
Sparse Core Ops, SparseCore 0:
  24.7 146.5 all-reduce.5
  188.6 141.8 all-reduce.7
  348.1 141.9 all-reduce.9
  507.8 141.9 all-reduce.11
  667.8 141.9 all-reduce.13
